TPU v7x, 128 devices: a whole 4x4x4 slice. The times are simulated.
128 devices in a mesh: row: 8 (over z, core), col: 16 (over y, x).
Axes of the slice: x: 4, y: 4, z: 4, core: 2. Of those that a mesh axis runs over, the one named last changes fastest.
Arguments:
- psi_val: float32 [64, 128, 128, 128], P(None, 'row', 'col'), may hold values from -6 to 6
- psi_cond: float32 [64, 128, 128, 128], P(None, 'row', 'col'), may hold values from -6 to 6
- eps_val: float32 [64], replicated, may hold values from -12 to -1
- eps_cond: float32 [64], replicated, may hold values from 1 to 12
- val_index: int32 [128], replicated, may hold values from 0 to 63
- cond_index: int32 [128], replicated, may hold values from 0 to 63
- gmap: int32 [8192], replicated, may hold values from 0 to 2097151, as said below
- chi0_in: float32 [2, 8192, 8192], P(None, 'row', 'col'), may hold values from -6 to 6
Outputs:
- chi0_out: float32 [2, 8192, 8192], P(None, 'row', 'col')
Inputs may be any that keep to these rules, and one draw needn't show every extreme that they name: gmap holds 8192 distinct entries. Entries g of device block d = g // 64 (d = r * 16 + c) have ky in [r * 16, (r + 1) * 16) and kz in [c * 8, (c + 1) * 8); kx is any.
All inputs are finite; a program needn't handle non-finite values.
Results may differ from a plain program's by a relative error of at most 0.000068.
Values sent between devices are 32-bit elements; how exact they have to be, the bound alone decides.
No kernel may reach another device: no remote copies, remote signals or barrier semaphores. Data moves between devices by JAX's collectives and lax.ppermute only.
A program may use at most 128 MiB of HBM per device.

v0:
```python
import math

import jax
import numpy as np
import jax.numpy as jnp
from jax import lax
from jax.sharding import PartitionSpec as P

GRID = 128
NG = 8192


HIGH = lax.Precision.HIGHEST


def phase_table(left, right, length):
    phase = left[:, None] * right[None, :] % length
    angle = phase.astype(jnp.float32) * (2.0 * math.pi / length)
    return (jnp.cos(angle), jnp.sin(angle))


def contract_pairs(left, right):
    return lax.dot_general(
        left, right, (((1,), (1,)), ((), ())), precision=HIGH, preferred_element_type=jnp.float32
    )


def on_device(psi_val, psi_cond, eps_val, eps_cond, val_index, cond_index, gmap, chi0_in):
    pairs = val_index.shape[0]
    scale = 1.0 / math.sqrt(GRID**3)
    row_pos = lax.axis_index("row")
    col_pos = lax.axis_index("col")
    mesh_cols = lax.axis_size("col")
    mesh_rows = lax.axis_size("row")
    per_device = NG // (mesh_rows * mesh_cols)
    row_span = GRID // mesh_rows
    col_span = GRID // mesh_cols
    steps = jnp.arange(GRID, dtype=jnp.int32)

    mirror = mesh_cols - 1 - col_pos
    low = jnp.minimum(col_pos, mirror)
    side = col_pos // (mesh_cols // 2)
    span_z = col_span + 1
    x_half = row_span // 2
    by_block = gmap.reshape(mesh_rows, mesh_cols, per_device)
    direct = lax.dynamic_index_in_dim(by_block, low, axis=1, keepdims=False)
    mirrored = lax.dynamic_index_in_dim(by_block, mesh_cols - 1 - low, axis=1, keepdims=False)
    both = jnp.stack([direct, mirrored], axis=1).reshape(-1)
    flip = (jnp.arange(both.shape[0], dtype=jnp.int32) // per_device) % 2
    freq_x = both // (GRID * GRID)
    freq_y = both // GRID % GRID
    freq_z = both % GRID
    freq_x = jnp.where(flip == 1, (GRID - freq_x) % GRID, freq_x)
    freq_y = jnp.where(flip == 1, (GRID - freq_y) % GRID, freq_y)
    freq_z = jnp.where(flip == 1, (GRID - freq_z) % GRID, freq_z) - low * col_span
    sign = jnp.where(flip == 1, -1.0, 1.0).astype(jnp.float32)
    pick = freq_y * span_z + freq_z
    x_glob = row_pos * row_span + side * x_half + jnp.arange(x_half, dtype=jnp.int32)
    cos_x, sin_x = phase_table(x_glob, freq_x, GRID)

    kz_set = (jnp.arange(mesh_cols // 2, dtype=jnp.int32)[:, None] * col_span
              + jnp.arange(span_z, dtype=jnp.int32)[None, :]).reshape(-1)
    cos_z, sin_z = phase_table(steps, kz_set, GRID)
    table_z = jnp.stack([cos_z, -sin_z], axis=-1).reshape(GRID, mesh_cols // 2, span_z, 2)
    table_z = jnp.stack([table_z, table_z[:, ::-1]], axis=0)
    cos_y, sin_y = phase_table(steps, steps, GRID)
    table_y = jnp.stack(
        [jnp.stack([cos_y, -sin_y], axis=-1), jnp.stack([sin_y, cos_y], axis=-1)], axis=1
    ).reshape(mesh_cols, col_span, 2, GRID, 2)

    sizes = [x_half // 4, x_half // 2, x_half // 4]
    pieces = []
    for i, chunk in enumerate(sizes):
        start = sum(sizes[:i])
        lo = slice(start, start + chunk)
        hi = slice(x_half + start, x_half + start + chunk)
        band_v = jnp.stack([psi_val[:, lo], psi_val[:, hi]], axis=1)
        band_c = jnp.stack([psi_cond[:, lo], psi_cond[:, hi]], axis=1)
        rho = jnp.take(band_v, val_index, axis=0, mode="clip") * jnp.take(
            band_c, cond_index, axis=0, mode="clip"
        )
        z_all = jnp.einsum("phxyz,hzcjt->hcpxyjt", rho, table_z, precision=HIGH)
        z_all = z_all.reshape((mesh_cols,) + z_all.shape[2:])
        z_mine = lax.all_to_all(z_all, "col", split_axis=0, concat_axis=0, tiled=True)
        if i >= 1:
            z_mine, pieces[i - 1] = lax.optimization_barrier((z_mine, pieces[i - 1]))
        y_all = jnp.einsum("spxyjt,syteu->ejuxp", z_mine, table_y, precision=HIGH)
        flat = y_all.reshape(GRID * span_z, 2 * chunk * pairs)
        chosen = jnp.take(flat, pick, axis=0, mode="clip").reshape(-1, 2, chunk, pairs)
        c_re = chosen[:, 0]
        c_im = chosen[:, 1]
        cx = cos_x[lo].T[:, :, None]
        sx = sin_x[lo].T[:, :, None]
        part_re = jnp.sum(c_re * cx + c_im * sx, axis=1)
        part_im = jnp.sum(c_im * cx - c_re * sx, axis=1)
        pieces.append(jnp.stack([part_re, part_im], axis=1))
    partial = pieces[0]
    for piece in pieces[1:]:
        partial = partial + piece
    partial = partial * jnp.stack([jnp.ones_like(sign), sign], axis=1)[:, :, None] * scale
    block = 2 * per_device
    spread = partial.reshape(mesh_rows, block, 2, pairs)
    gathered = lax.all_to_all(spread, "row", split_axis=0, concat_axis=0, tiled=True)
    both_blocks = jnp.sum(gathered, axis=0).reshape(2, per_device, 2, pairs)
    mine = lax.dynamic_index_in_dim(both_blocks, side, axis=0, keepdims=False)
    theirs = lax.dynamic_index_in_dim(both_blocks, 1 - side, axis=0, keepdims=False)
    partner = lax.ppermute(theirs, "col", [(c, mesh_cols - 1 - c) for c in range(mesh_cols)])
    own = mine + partner
    copies = jnp.broadcast_to(own[None], (mesh_cols,) + own.shape)
    row_blocks = lax.all_to_all(copies, "col", split_axis=0, concat_axis=0, tiled=True)
    rows = row_blocks.reshape(mesh_cols * per_device, 2, pairs)
    half = mesh_cols // 2
    send = lax.dynamic_slice_in_dim(rows, (col_pos // half) * half * per_device, half * per_device, 0)
    perm = []
    for src_r in range(mesh_rows):
        for src_c in range(mesh_cols):
            dst_r = src_c % half
            dst_c = 2 * src_r + src_c // half
            perm.append((src_r * mesh_cols + src_c, dst_r * mesh_cols + dst_c))
    cols = lax.ppermute(send, ("row", "col"), perm)

    val_hot = val_index[:, None] == jnp.arange(eps_val.shape[0], dtype=jnp.int32)[None, :]
    cond_hot = cond_index[:, None] == jnp.arange(eps_cond.shape[0], dtype=jnp.int32)[None, :]
    energy_v = jnp.sum(jnp.where(val_hot, eps_val[None, :], 0.0), axis=1)
    energy_c = jnp.sum(jnp.where(cond_hot, eps_cond[None, :], 0.0), axis=1)
    weight = (-6.0 / (math.sqrt(pairs) * (energy_c - energy_v)))[None, :]
    rows_re = rows[:, 0]
    rows_im = rows[:, 1]
    cols_re = cols[:, 0]
    cols_im = cols[:, 1]
    out_re = (
        chi0_in[0]
        + contract_pairs(weight * rows_re, cols_re)
        + contract_pairs(weight * rows_im, cols_im)
    )
    out_im = (
        chi0_in[1]
        + contract_pairs(weight * rows_im, cols_re)
        - contract_pairs(weight * rows_re, cols_im)
    )
    return jnp.stack([out_re, out_im])


def solution(mesh):
    return jax.shard_map(
        on_device,
        mesh=mesh,
        in_specs=(
            P(None, "row", "col", None),
            P(None, "row", "col", None),
            P(),
            P(),
            P(),
            P(),
            P(),
            P(None, "row", "col"),
        ),
        out_specs=P(None, "row", "col"),
        check_vma=False,
    )
```

profile of v0, /device:TPU:24, one launch (start us, length us, event | category | flops | bytes accessed | tf_op | source)
XLA Modules:
  0.0 356.8 jit_solution(15113770850506737179)
XLA Ops:
  6.3 2.0 gather_fusion.2
  8.3 2.3 pad_maximum_fusion.4
  10.6 2.0 gather_fusion.3
  12.6 2.7 multiply_bitcast_fusion.2
  15.3 4.6 %fusion.18 = f32[2,8,9,2,128,2,8]{4,2,6,5,3,1,0:T(8,128)S(1)} fusion(f32[128,2,2,8,128,1,1]{4,3,2,1,0,6,5:T(8,128)S(1)} %multiply_bitcast_fusion.2, f32[1,128,8,9,2]{1,3,4,2,0:T(8,128)S(1)} %reverse_bitcast_fusion, f32[1,128,8,9,1]{1,3,4,2,0:T(8,128)S(1)} %get-tuple-element.49, f32[1,128,8,9,1]{1,3,4,2,0:T(8,128)S(1)} %get-tuple-element.48), kind=kOutput, calls=%fused_computation.32 | convolution fusion | flops 906043392 | bytes 4603904 | tf_op jit(solution)/shard_map/phxyz,hzcjt->hcpxyjt/dot_general | solution.py:82
  19.9 2.4 copy.100
  22.3 7.3 %all-to-all-start.1 = ((f32[16,128,2,8,9,2]{1,3,5,4,2,0:T(8,128)}), f32[16,128,2,8,9,2]{1,3,5,4,2,0:T(8,128)}, u32[]{:S(2)}, u32[]{:S(2)}) async-start(f32[16,128,2,8,9,2]{1,3,5,4,2,0:T(8,128)} %copy.100), calls=%async_computation.1 | async-start | bytes 4718592 | tf_op jit(solution)/shard_map/all_to_all | solution.py:84
  31.5 2.8 gather_fusion
  36.3 2.9 gather_fusion.1
  39.2 4.5 %multiply_bitcast_fusion = f32[128,2,4,8,128,1,1]{4,3,2,1,0,6,5:T(8,128)S(1)} fusion(f32[128,2,4,8,128]{4,3,2,1,0:T(8,128)} %gather_fusion, f32[128,2,4,8,128]{4,3,2,1,0:T(8,128)} %gather_fusion.1), kind=kLoop, calls=%fused_computation.15 | loop fusion | flops 1048576 | bytes 12582912 | tf_op jit(solution)/shard_map/mul | solution.py:79
  43.6 9.0 %fusion.3 = f32[2,8,9,2,128,4,8]{4,2,6,5,3,1,0:T(8,128)S(1)} fusion(f32[128,2,4,8,128,1,1]{4,3,2,1,0,6,5:T(8,128)S(1)} %multiply_bitcast_fusion, f32[1,128,8,9,2]{1,3,4,2,0:T(8,128)S(1)} %reverse_bitcast_fusion, f32[1,128,8,9,1]{1,3,4,2,0:T(8,128)S(1)} %get-tuple-element.49, f32[1,128,8,9,1]{1,3,4,2,0:T(8,128)S(1)} %get-tuple-element.48), kind=kOutput, calls=%fused_computation.13 | convolution fusion | flops 1812013056 | bytes 9060352 | tf_op jit(solution)/shard_map/phxyz,hzcjt->hcpxyjt/dot_general | solution.py:82
  52.7 4.5 %copy.98 = f32[16,128,4,8,9,2]{1,3,5,4,2,0:T(8,128)} copy(f32[16,128,4,8,9,2]{1,4,3,2,5,0:T(8,128)S(1)} %bitcast.188) | data formatting | bytes 9437184 | tf_op jit(solution)/shard_map/reshape | solution.py:83
  57.2 6.5 %all-to-all-done.1 = f32[16,128,2,8,9,2]{1,3,5,4,2,0:T(8,128)} async-done(((f32[16,128,2,8,9,2]{1,3,5,4,2,0:T(8,128)}), f32[16,128,2,8,9,2]{1,3,5,4,2,0:T(8,128)}, u32[]{:S(2)}, u32[]{:S(2)}) %all-to-all-start.1) | async-done | bytes 2359328 | tf_op jit(solution)/shard_map/all_to_all | solution.py:84
  63.7 5.9 %all-to-all-start = ((f32[16,128,4,8,9,2]{1,3,5,4,2,0:T(8,128)}), f32[16,128,4,8,9,2]{1,3,5,4,2,0:T(8,128)}, u32[]{:S(2)}, u32[]{:S(2)}) async-start(f32[16,128,4,8,9,2]{1,3,5,4,2,0:T(8,128)} %copy.98), calls=%async_computation | async-start | bytes 9437184 | tf_op jit(solution)/shard_map/all_to_all | solution.py:84
  73.9 2.1 multiply_bitcast_fusion.1
  75.9 4.6 %fusion.16 = f32[2,8,9,2,128,2,8]{4,2,6,5,3,1,0:T(8,128)S(1)} fusion(f32[128,2,2,8,128,1,1]{4,3,2,1,0,6,5:T(8,128)S(1)} %multiply_bitcast_fusion.1, f32[1,128,8,9,2]{1,3,4,2,0:T(8,128)S(1)} %reverse_bitcast_fusion, f32[1,128,8,9,1]{1,3,4,2,0:T(8,128)S(1)} %get-tuple-element.49, f32[1,128,8,9,1]{1,3,4,2,0:T(8,128)S(1)} %get-tuple-element.48), kind=kOutput, calls=%fused_computation.30 | convolution fusion | flops 906043392 | bytes 4603904 | tf_op jit(solution)/shard_map/phxyz,hzcjt->hcpxyjt/dot_general | solution.py:82
  80.5 2.4 copy.105
  83.5 2.1 fusion.34
  86.9 50.3 %all-to-all-done = f32[16,128,4,8,9,2]{1,3,5,4,2,0:T(8,128)} async-done(((f32[16,128,4,8,9,2]{1,3,5,4,2,0:T(8,128)}), f32[16,128,4,8,9,2]{1,3,5,4,2,0:T(8,128)}, u32[]{:S(2)}, u32[]{:S(2)}) %all-to-all-start) | async-done | bytes 4718624 | tf_op jit(solution)/shard_map/all_to_all | solution.py:84
  137.2 6.6 %all-to-all-start.2 = ((f32[16,128,2,8,9,2]{1,3,5,4,2,0:T(8,128)}), f32[16,128,2,8,9,2]{1,3,5,4,2,0:T(8,128)}, u32[]{:S(2)}, u32[]{:S(2)}) async-start(f32[16,128,2,8,9,2]{1,3,5,4,2,0:T(8,128)} %copy.105), calls=%async_computation.2 | async-start | bytes 4718592 | tf_op jit(solution)/shard_map/all_to_all | solution.py:84
  145.1 5.1 %fusion.22 = f32[128,9,2,2,128]{4,0,1,3,2:T(8,128)S(1)} fusion(f32[16,128,2,8,9,2]{1,3,5,4,2,0:T(8,128)} %all-to-all-done.1, f32[16,8,1,128,1]{3,0,1,2,4:T(8,128)S(1)} %get-tuple-element.47, f32[16,8,1,128,1]{3,0,1,2,4:T(8,128)S(1)} %get-tuple-element.46, f32[16,8,1,128,1]{3,0,1,2,4:T(8,128)S(1)} %get-tuple-element.45), kind=kOutput, calls=%fused_computation.41 | convolution fusion | flops 1812135936 | bytes 4915200 | tf_op jit(solution)/shard_map/spxyjt,syteu->ejuxp/dot_general | solution.py:87
  150.2 3.2 copy.102
  153.5 3.3 reshape.718
  156.7 4.9 %gather_fusion.4 = f32[1024,512]{1,0:T(8,128)} fusion(f32[1152,512]{1,0:T(8,128)S(1)} %reshape.718, s32[1024]{0:T(1024)S(1)} %broadcast_clamp_fusion), kind=kCustom, calls=%fused_computation.4 | custom fusion | bytes 4198400 | tf_op jit(solution)/shard_map/jit(_take)/gather | solution.py:89
  161.6 2.6 reshape.721
  164.2 6.3 %add_reduce_fusion.2 = (f32[1024,128]{1,0:T(8,128)S(1)}, f32[1024,128]{1,0:T(8,128)S(1)}) fusion(f32[1024,2,2,128]{3,2,1,0:T(2,128)S(1)} %reshape.721, f32[1024,2]{1,0:T(8,128)S(1)} %get-tuple-element.40, f32[1024,2]{1,0:T(8,128)S(1)} %get-tuple-element.56), kind=kLoop, calls=%fused_computation.59 | loop fusion | flops 1835008 | bytes 3162112 | tf_op jit(solution)/shard_map/reduce_sum | solution.py:94
  171.3 9.6 %fusion.11 = f32[128,9,2,4,128]{4,0,1,3,2:T(8,128)S(1)} fusion(f32[16,128,4,8,9,2]{1,3,5,4,2,0:T(8,128)} %all-to-all-done, f32[16,8,1,128,1]{3,0,1,2,4:T(8,128)S(1)} %copy-done.7, f32[16,8,1,128,1]{3,0,1,2,4:T(8,128)S(1)} %get-tuple-element.46, f32[16,8,1,128,1]{3,0,1,2,4:T(8,128)S(1)} %get-tuple-element.45), kind=kOutput, calls=%fused_computation.22 | convolution fusion | flops 3624075264 | bytes 9633792 | tf_op jit(solution)/shard_map/spxyjt,syteu->ejuxp/dot_general | solution.py:87
  181.0 5.2 %copy.107 = f32[128,9,2,4,128]{4,3,2,1,0:T(4,128)} copy(f32[128,9,2,4,128]{4,0,1,3,2:T(8,128)S(1)} %fusion.11) | data formatting | bytes 9437184 | tf_op jit(solution)/shard_map/spxyjt,syteu->ejuxp/transpose | solution.py:87
  186.2 6.5 %reshape.724 = f32[1152,1024]{1,0:T(8,128)} reshape(f32[128,9,2,4,128]{4,3,2,1,0:T(4,128)} %copy.107) | data formatting | bytes 9437184 | tf_op jit(solution)/shard_map/reshape | solution.py:88
  192.7 8.7 %gather_fusion.7 = f32[1024,1024]{1,0:T(8,128)} fusion(f32[1152,1024]{1,0:T(8,128)} %reshape.724, s32[1024]{0:T(1024)S(1)} %broadcast_clamp_fusion), kind=kCustom, calls=%fused_computation.7 | custom fusion | bytes 8392704 | tf_op jit(solution)/shard_map/jit(_take)/gather | solution.py:89
  201.4 5.7 %reshape.725 = f32[1024,2,4,128]{3,2,1,0:T(4,128)} reshape(f32[1024,1024]{1,0:T(8,128)} %gather_fusion.7) | data formatting | bytes 8388608 | tf_op jit(solution)/shard_map/reshape | solution.py:89
  207.1 8.1 %add_reduce_fusion = (f32[1024,128]{1,0:T(8,128)S(1)}, f32[1024,128]{1,0:T(8,128)S(1)}) fusion(f32[1024,2,4,128]{3,2,1,0:T(4,128)} %reshape.725, f32[1024,4]{1,0:T(8,128)S(1)} %copy-done.4, f32[1024,4]{1,0:T(8,128)S(1)} %copy-done.5), kind=kLoop, calls=%fused_computation.38 | loop fusion | flops 3932160 | bytes 5275648 | tf_op jit(solution)/shard_map/reduce_sum | solution.py:94
  216.3 5.1 %fusion.25 = f32[128,9,2,2,128]{4,0,1,3,2:T(8,128)S(1)} fusion(f32[16,128,2,8,9,2]{1,3,5,4,2,0:T(8,128)} %all-to-all-done.2, f32[16,8,1,128,1]{3,0,1,2,4:T(8,128)S(1)} %copy-done.7, f32[16,8,1,128,1]{3,0,1,2,4:T(8,128)S(1)} %get-tuple-element.46, f32[16,8,1,128,1]{3,0,1,2,4:T(8,128)S(1)} %get-tuple-element.45), kind=kOutput, calls=%fused_computation.42 | convolution fusion | flops 1812135936 | bytes 4915200 | tf_op jit(solution)/shard_map/spxyjt,syteu->ejuxp/dot_general | solution.py:87
  221.4 3.2 copy.110
  224.7 3.3 reshape.726
  227.9 4.9 %gather_fusion.8 = f32[1024,512]{1,0:T(8,128)} fusion(f32[1152,512]{1,0:T(8,128)S(1)} %reshape.726, s32[1024]{0:T(1024)S(1)} %broadcast_clamp_fusion), kind=kCustom, calls=%fused_computation.8 | custom fusion | bytes 4198400 | tf_op jit(solution)/shard_map/jit(_take)/gather | solution.py:89
  232.8 2.6 reshape.727
  235.4 7.9 %add_reduce_fusion.1 = (f32[1024,128]{1,0:T(8,128)S(1)}, f32[1024,128]{1,0:T(8,128)S(1)}) fusion(f32[1024,2,2,128]{3,2,1,0:T(2,128)S(1)} %reshape.727, f32[1024,2]{1,0:T(8,128)} %get-tuple-element.39, f32[1024,2]{1,0:T(8,128)} %get-tuple-element.57), kind=kLoop, calls=%fused_computation.57 | loop fusion | flops 1835008 | bytes 3162112 | tf_op jit(solution)/shard_map/reduce_sum | solution.py:94
  244.8 5.3 %all-to-all-start.3 = ((f32[8,128,2,128]{3,1,2,0:T(8,128)}), f32[8,128,2,128]{3,1,2,0:T(8,128)S(1)}, u32[]{:S(2)}, u32[]{:S(2)}) async-start(f32[8,128,2,128]{3,1,2,0:T(8,128)} %copy.112), calls=%async_computation.3 | async-start | bytes 2097152 | tf_op jit(solution)/shard_map/all_to_all | solution.py:103
  250.1 16.0 %all-to-all-done.3 = f32[8,128,2,128]{3,1,2,0:T(8,128)S(1)} async-done(((f32[8,128,2,128]{3,1,2,0:T(8,128)}), f32[8,128,2,128]{3,1,2,0:T(8,128)S(1)}, u32[]{:S(2)}, u32[]{:S(2)}) %all-to-all-start.3) | async-done | bytes 1048608 | tf_op jit(solution)/shard_map/all_to_all | solution.py:103
  266.1 2.7 collective-permute-start
  268.9 4.9 %collective-permute-done = f32[64,2,128]{2,0,1:T(8,128)S(1)} collective-permute-done((f32[64,2,128]{2,0,1:T(8,128)S(1)}, f32[64,2,128]{2,0,1:T(8,128)S(1)}, u32[]{:S(2)}, u32[]{:S(2)}) %collective-permute-start) | collective-permute-done | bytes 65568 | tf_op jit(solution)/shard_map/ppermute | solution.py:107
  275.3 6.6 %all-to-all-start.4 = ((f32[16,64,2,128]{3,2,1,0:T(2,128)}), f32[16,64,2,128]{3,2,1,0:T(2,128)S(1)}, u32[]{:S(2)}, u32[]{:S(2)}) async-start(f32[16,64,2,128]{3,2,1,0:T(2,128)} %broadcast_in_dim.77), calls=%async_computation.4 | async-start | bytes 2097152 | tf_op jit(solution)/shard_map/all_to_all | solution.py:110
  281.9 13.6 %all-to-all-done.4 = f32[16,64,2,128]{3,2,1,0:T(2,128)S(1)} async-done(((f32[16,64,2,128]{3,2,1,0:T(2,128)}), f32[16,64,2,128]{3,2,1,0:T(2,128)S(1)}, u32[]{:S(2)}, u32[]{:S(2)}) %all-to-all-start.4) | async-done | bytes 1048608 | tf_op jit(solution)/shard_map/all_to_all | solution.py:110
  295.5 5.0 %collective-permute-start.1 = (f32[512,2,128]{2,1,0:T(2,128)S(1)}, f32[512,2,128]{2,1,0:T(2,128)S(1)}, u32[]{:S(2)}, u32[]{:S(2)}) collective-permute-start(f32[512,2,128]{2,1,0:T(2,128)S(1)} %constant_dynamic-slice_fusion), channel_id=1, source_target_pairs={{0,0},{1,16},{2,32},{3,48},{4,64},{5,80},{6,96},{7,112},{8,1},{9,1... | collective-permute-start | bytes 1572872 | tf_op jit(solution)/shard_map/ppermute | solution.py:120
  301.4 44.9 %collective-permute-done.1 = f32[512,2,128]{2,1,0:T(2,128)S(1)} collective-permute-done((f32[512,2,128]{2,1,0:T(2,128)S(1)}, f32[512,2,128]{2,1,0:T(2,128)S(1)}, u32[]{:S(2)}, u32[]{:S(2)}) %collective-permute-start.1) | collective-permute-done | bytes 524320 | tf_op jit(solution)/shard_map/ppermute | solution.py:120
  352.2 2.1 fusion.21
  354.3 2.0 copy-done.15
  (82 shorter events, 29.0 us)
Async XLA Ops:
  2.1 2.8 copy-start.2
  22.3 41.4 %all-to-all-start.1 = ((f32[16,128,2,8,9,2]{1,3,5,4,2,0:T(8,128)}), f32[16,128,2,8,9,2]{1,3,5,4,2,0:T(8,128)}, u32[]{:S(2)}, u32[]{:S(2)}) async-start(f32[16,128,2,8,9,2]{1,3,5,4,2,0:T(8,128)} %copy.100), calls=%async_computation.1 | async-start | bytes 4718592 | tf_op jit(solution)/shard_map/all_to_all | solution.py:84
  57.2 12.4 %copy-start.9 = (s32[8192]{0:T(1024)S(1)}, s32[8192]{0:T(1024)}, u32[]{:S(2)}) copy-start(s32[8192]{0:T(1024)} %param.14) | copy-start | bytes 98308
  63.7 73.5 %all-to-all-start = ((f32[16,128,4,8,9,2]{1,3,5,4,2,0:T(8,128)}), f32[16,128,4,8,9,2]{1,3,5,4,2,0:T(8,128)}, u32[]{:S(2)}, u32[]{:S(2)}) async-start(f32[16,128,4,8,9,2]{1,3,5,4,2,0:T(8,128)} %copy.98), calls=%async_computation | async-start | bytes 9437184 | tf_op jit(solution)/shard_map/all_to_all | solution.py:84
  69.9 2.0 copy-start
  71.9 2.0 copy-start.1
  83.4 61.7 %copy-start.6 = (f32[16,8,1,128,1]{3,0,1,2,4:T(8,128)}, f32[16,8,1,128,1]{3,0,1,2,4:T(8,128)S(1)}, u32[]{:S(2)}) copy-start(f32[16,8,1,128,1]{3,0,1,2,4:T(8,128)S(1)} %get-tuple-element.47) | copy-start | bytes 196612
  137.2 79.1 %all-to-all-start.2 = ((f32[16,128,2,8,9,2]{1,3,5,4,2,0:T(8,128)}), f32[16,128,2,8,9,2]{1,3,5,4,2,0:T(8,128)}, u32[]{:S(2)}, u32[]{:S(2)}) async-start(f32[16,128,2,8,9,2]{1,3,5,4,2,0:T(8,128)} %copy.105), calls=%async_computation.2 | async-start | bytes 4718592 | tf_op jit(solution)/shard_map/all_to_all | solution.py:84
  170.5 0.8 copy-start.7
  201.4 5.7 %copy-start.4 = (f32[1024,4]{1,0:T(8,128)S(1)}, f32[1024,4]{1,0:T(8,128)}, u32[]{:S(2)}) copy-start(f32[1024,4]{1,0:T(8,128)} %get-tuple-element.58) | copy-start | bytes 49156
  201.4 5.7 %copy-start.5 = (f32[1024,4]{1,0:T(8,128)S(1)}, f32[1024,4]{1,0:T(8,128)}, u32[]{:S(2)}) copy-start(f32[1024,4]{1,0:T(8,128)} %get-tuple-element.59) | copy-start | bytes 49156
  235.4 7.9 %copy-start.3 = (f32[1024,2,128]{2,0,1:T(8,128)S(1)}, f32[1024,2,128]{2,0,1:T(8,128)}, u32[]{:S(2)}) copy-start(f32[1024,2,128]{2,0,1:T(8,128)} %pad_maximum_fusion.8) | copy-start | bytes 3145732
  244.8 21.3 %all-to-all-start.3 = ((f32[8,128,2,128]{3,1,2,0:T(8,128)}), f32[8,128,2,128]{3,1,2,0:T(8,128)S(1)}, u32[]{:S(2)}, u32[]{:S(2)}) async-start(f32[8,128,2,128]{3,1,2,0:T(8,128)} %copy.112), calls=%async_computation.3 | async-start | bytes 2097152 | tf_op jit(solution)/shard_map/all_to_all | solution.py:103
  266.1 7.7 %collective-permute-start = (f32[64,2,128]{2,0,1:T(8,128)S(1)}, f32[64,2,128]{2,0,1:T(8,128)S(1)}, u32[]{:S(2)}, u32[]{:S(2)}) collective-permute-start(f32[64,2,128]{2,0,1:T(8,128)S(1)} %dynamic-slice_bitcast_fusion), channel_id=1, source_target_pairs={{0,15},{1,14},{2,13},{3,12},{4,11},{5,10},{6,9},{7,8},{8,7},{9,6},... | collective-permute-start | bytes 196616 | tf_op jit(solution)/shard_map/ppermute | solution.py:107
  273.9 26.7 %copy-start.10 = (s32[128]{0:T(128)S(1)}, s32[128]{0:T(128)}, u32[]{:S(2)}) copy-start(s32[128]{0:T(128)} %param.12) | copy-start | bytes 1540
  273.9 26.7 %copy-start.11 = (s32[128]{0:T(128)S(1)}, s32[128]{0:T(128)}, u32[]{:S(2)}) copy-start(s32[128]{0:T(128)} %param.13) | copy-start | bytes 1540
  273.9 26.7 %copy-start.12 = (f32[64]{0:T(128)S(1)}, f32[64]{0:T(128)}, u32[]{:S(2)}) copy-start(f32[64]{0:T(128)} %param.10) | copy-start | bytes 772
  273.9 26.6 %copy-start.13 = (f32[64]{0:T(128)S(1)}, f32[64]{0:T(128)}, u32[]{:S(2)}) copy-start(f32[64]{0:T(128)} %param.11) | copy-start | bytes 772
  275.3 20.2 %all-to-all-start.4 = ((f32[16,64,2,128]{3,2,1,0:T(2,128)}), f32[16,64,2,128]{3,2,1,0:T(2,128)S(1)}, u32[]{:S(2)}, u32[]{:S(2)}) async-start(f32[16,64,2,128]{3,2,1,0:T(2,128)} %broadcast_in_dim.77), calls=%async_computation.4 | async-start | bytes 2097152 | tf_op jit(solution)/shard_map/all_to_all | solution.py:110
  295.5 50.8 %collective-permute-start.1 = (f32[512,2,128]{2,1,0:T(2,128)S(1)}, f32[512,2,128]{2,1,0:T(2,128)S(1)}, u32[]{:S(2)}, u32[]{:S(2)}) collective-permute-start(f32[512,2,128]{2,1,0:T(2,128)S(1)} %constant_dynamic-slice_fusion), channel_id=1, source_target_pairs={{0,0},{1,16},{2,32},{3,48},{4,64},{5,80},{6,96},{7,112},{8,1},{9,1... | collective-permute-start | bytes 1572872 | tf_op jit(solution)/shard_map/ppermute | solution.py:120
  346.7 5.4 %copy-start.14 = (f32[2,1024,512]{2,1,0:T(8,128)S(1)}, f32[2,1024,512]{2,1,0:T(8,128)}, u32[]{:S(2)}) copy-start(f32[2,1024,512]{2,1,0:T(8,128)} %custom-call.18) | copy-start | bytes 12582916
  348.5 3.6 %copy-start.8 = (f32[2,1024,512]{2,1,0:T(8,128)S(1)}, f32[2,1024,512]{2,1,0:T(8,128)}, u32[]{:S(2)}) copy-start(f32[2,1024,512]{2,1,0:T(8,128)} %param.15) | copy-start | bytes 12582916
  354.3 2.0 copy-start.15
where the time goes:
time: 364 us; the launch traced here: 357 us
  waiting for transfers between devices  136 us (37%)
  local copies, waits for them, and re-layouts  93.1 us (26%)
  matrix products  45.5 us (12%)
  other arithmetic  41.6 us (11%)
  starting transfers between devices  39.4 us (11%)
    all_to_all x3, waiting for transfers between devices, on_device(): lax.all_to_all(z_all, 'col', split_axis=0, concat_axis=0, tiled=True)  56.8 us
    ppermute x1, waiting for transfers between devices, on_device(): cols = lax.ppermute(send, ('row', 'col'), perm)  44.9 us
    reduce_sum x3, other arithmetic, on_device(): part_re = jnp.sum(c_re * cx + c_im * sx, axis=1)  22.4 us
    dot_general x3, matrix products, on_device(): y_all = jnp.einsum('spxyjt,syteu->ejuxp', z_mine, table_y, precision=HIGH)  19.9 us
    all_to_all x3, starting transfers between devices, on_device(): lax.all_to_all(z_all, 'col', split_axis=0, concat_axis=0, tiled=True)  19.8 us
    gather x3, local copies, waits for them, and re-layouts, on_device(): jnp.take(flat, pick, axis=0, mode='clip').reshape(-1, 2, chunk, pairs)  18.4 us
    dot_general x3, matrix products, on_device(): z_all = jnp.einsum('phxyz,hzcjt->hcpxyjt', rho, table_z, precision=HIGH)  18.1 us
    all_to_all x1, waiting for transfers between devices, on_device(): lax.all_to_all(spread, 'row', split_axis=0, concat_axis=0, tiled=True)  16 us
  transfers between devices with their start and end apart: 7, of which 6 were waited for; matrix products, arithmetic and copies ran while one was open for 33% of the time, Pallas kernels for 0%

commit v1 on v0

--- a/solution.py
+++ b/solution.py
@@ -85,8 +85,8 @@
         if i >= 1:
             z_mine, pieces[i - 1] = lax.optimization_barrier((z_mine, pieces[i - 1]))
         y_all = jnp.einsum("spxyjt,syteu->ejuxp", z_mine, table_y, precision=HIGH)
-        flat = y_all.reshape(GRID * span_z, 2 * chunk * pairs)
-        chosen = jnp.take(flat, pick, axis=0, mode="clip").reshape(-1, 2, chunk, pairs)
+        flat = y_all.reshape(GRID * span_z, 2, chunk, pairs)
+        chosen = jnp.take(flat, pick, axis=0, mode="clip")
         c_re = chosen[:, 0]
         c_im = chosen[:, 1]
         cx = cos_x[lo].T[:, :, None]

time: 364 us -> 352 us (0.967)
  local copies, waits for them, and re-layouts: 93.1 us -> 81 us
    reshape x6 -> x0, local copies, waits for them, and re-layouts: 23.9 us -> none  [the longest x3 13 us: on_device(): flat = y_all.reshape(GRID * span_z, 2 * chunk * pairs)]
    gather x3, local copies, waits for them, and re-layouts: 18.4 us -> 31.3 us  [on_device(): chosen = jnp.take(flat, pick, axis=0, mode='clip')]
  transfers between devices with their start and end apart: 7 -> 7, of which waited for: 6 -> 6; matrix products, arithmetic and copies ran while one was open for 33% -> 32% of each run, Pallas kernels for 0% -> 0%
where the time goes in v1:
time: 352 us; the launch traced here: 345 us
  waiting for transfers between devices  135 us (38%)
  local copies, waits for them, and re-layouts  81 us (23%)
  matrix products  45.1 us (13%)
  other arithmetic  43.8 us (12%)
  starting transfers between devices  38.9 us (11%)
    all_to_all x3, waiting for transfers between devices, on_device(): lax.all_to_all(z_all, 'col', split_axis=0, concat_axis=0, tiled=True)  55.8 us
    ppermute x1, waiting for transfers between devices, on_device(): cols = lax.ppermute(send, ('row', 'col'), perm)  45.2 us
    gather x3, local copies, waits for them, and re-layouts, on_device(): chosen = jnp.take(flat, pick, axis=0, mode='clip')  31.3 us
    reduce_sum x3, other arithmetic, on_device(): part_re = jnp.sum(c_re * cx + c_im * sx, axis=1)  24 us
    all_to_all x3, starting transfers between devices, on_device(): lax.all_to_all(z_all, 'col', split_axis=0, concat_axis=0, tiled=True)  19.5 us
    dot_general x3, matrix products, on_device(): y_all = jnp.einsum('spxyjt,syteu->ejuxp', z_mine, table_y, precision=HIGH)  19.4 us
    dot_general x3, matrix products, on_device(): z_all = jnp.einsum('phxyz,hzcjt->hcpxyjt', rho, table_z, precision=HIGH)  18.1 us
    all_to_all x1, waiting for transfers between devices, on_device(): lax.all_to_all(spread, 'row', split_axis=0, concat_axis=0, tiled=True)  16 us
  transfers between devices with their start and end apart: 7, of which 6 were waited for; matrix products, arithmetic and copies ran while one was open for 32% of the time, Pallas kernels for 0%

profile of v1, /device:TPU:24, one launch (start us, length us, event | category | flops | bytes accessed | tf_op | source)
XLA Modules:
  0.0 345.2 jit_solution(7332225661745146061)
XLA Ops:
  2.1 1.8 slice_bitcast_fusion.23
  6.3 2.0 gather_fusion.2
  8.3 2.3 pad_maximum_fusion.4
  10.6 2.0 gather_fusion.3
  12.6 2.7 multiply_bitcast_fusion.2
  15.3 4.6 %fusion.18 = f32[2,8,9,2,128,2,8]{4,2,6,5,3,1,0:T(8,128)S(1)} fusion(f32[128,2,2,8,128,1,1]{4,3,2,1,0,6,5:T(8,128)S(1)} %multiply_bitcast_fusion.2, f32[1,128,8,9,2]{1,3,4,2,0:T(8,128)S(1)} %reverse_bitcast_fusion, f32[1,128,8,9,1]{1,3,4,2,0:T(8,128)S(1)} %get-tuple-element.49, f32[1,128,8,9,1]{1,3,4,2,0:T(8,128)S(1)} %get-tuple-element.48), kind=kOutput, calls=%fused_computation.32 | convolution fusion | flops 906043392 | bytes 4603904 | tf_op jit(solution)/shard_map/phxyz,hzcjt->hcpxyjt/dot_general | solution.py:82
  19.9 2.4 copy.100
  22.2 7.4 %all-to-all-start.1 = ((f32[16,128,2,8,9,2]{1,3,5,4,2,0:T(8,128)}), f32[16,128,2,8,9,2]{1,3,5,4,2,0:T(8,128)}, u32[]{:S(2)}, u32[]{:S(2)}) async-start(f32[16,128,2,8,9,2]{1,3,5,4,2,0:T(8,128)} %copy.100), calls=%async_computation.1 | async-start | bytes 4718592 | tf_op jit(solution)/shard_map/all_to_all | solution.py:84
  31.5 2.8 gather_fusion
  36.3 2.8 gather_fusion.1
  39.0 4.5 %multiply_bitcast_fusion = f32[128,2,4,8,128,1,1]{4,3,2,1,0,6,5:T(8,128)S(1)} fusion(f32[128,2,4,8,128]{4,3,2,1,0:T(8,128)} %gather_fusion, f32[128,2,4,8,128]{4,3,2,1,0:T(8,128)} %gather_fusion.1), kind=kLoop, calls=%fused_computation.15 | loop fusion | flops 1048576 | bytes 12582912 | tf_op jit(solution)/shard_map/mul | solution.py:79
  43.5 9.0 %fusion.3 = f32[2,8,9,2,128,4,8]{4,2,6,5,3,1,0:T(8,128)S(1)} fusion(f32[128,2,4,8,128,1,1]{4,3,2,1,0,6,5:T(8,128)S(1)} %multiply_bitcast_fusion, f32[1,128,8,9,2]{1,3,4,2,0:T(8,128)S(1)} %reverse_bitcast_fusion, f32[1,128,8,9,1]{1,3,4,2,0:T(8,128)S(1)} %get-tuple-element.49, f32[1,128,8,9,1]{1,3,4,2,0:T(8,128)S(1)} %get-tuple-element.48), kind=kOutput, calls=%fused_computation.13 | convolution fusion | flops 1812013056 | bytes 9060352 | tf_op jit(solution)/shard_map/phxyz,hzcjt->hcpxyjt/dot_general | solution.py:82
  52.5 4.8 %copy.98 = f32[16,128,4,8,9,2]{1,3,5,4,2,0:T(8,128)} copy(f32[16,128,4,8,9,2]{1,4,3,2,5,0:T(8,128)S(1)} %bitcast.191) | data formatting | bytes 9437184 | tf_op jit(solution)/shard_map/reshape | solution.py:83
  57.3 6.3 %all-to-all-done.1 = f32[16,128,2,8,9,2]{1,3,5,4,2,0:T(8,128)} async-done(((f32[16,128,2,8,9,2]{1,3,5,4,2,0:T(8,128)}), f32[16,128,2,8,9,2]{1,3,5,4,2,0:T(8,128)}, u32[]{:S(2)}, u32[]{:S(2)}) %all-to-all-start.1) | async-done | bytes 2359328 | tf_op jit(solution)/shard_map/all_to_all | solution.py:84
  63.6 5.8 %all-to-all-start = ((f32[16,128,4,8,9,2]{1,3,5,4,2,0:T(8,128)}), f32[16,128,4,8,9,2]{1,3,5,4,2,0:T(8,128)}, u32[]{:S(2)}, u32[]{:S(2)}) async-start(f32[16,128,4,8,9,2]{1,3,5,4,2,0:T(8,128)} %copy.98), calls=%async_computation | async-start | bytes 9437184 | tf_op jit(solution)/shard_map/all_to_all | solution.py:84
  69.7 2.0 gather_fusion.5
  71.8 2.0 gather_fusion.6
  73.7 2.1 multiply_bitcast_fusion.1
  75.8 4.6 %fusion.16 = f32[2,8,9,2,128,2,8]{4,2,6,5,3,1,0:T(8,128)S(1)} fusion(f32[128,2,2,8,128,1,1]{4,3,2,1,0,6,5:T(8,128)S(1)} %multiply_bitcast_fusion.1, f32[1,128,8,9,2]{1,3,4,2,0:T(8,128)S(1)} %reverse_bitcast_fusion, f32[1,128,8,9,1]{1,3,4,2,0:T(8,128)S(1)} %get-tuple-element.49, f32[1,128,8,9,1]{1,3,4,2,0:T(8,128)S(1)} %get-tuple-element.48), kind=kOutput, calls=%fused_computation.30 | convolution fusion | flops 906043392 | bytes 4603904 | tf_op jit(solution)/shard_map/phxyz,hzcjt->hcpxyjt/dot_general | solution.py:82
  80.4 2.4 copy.105
  83.9 2.1 fusion.34
  87.6 49.5 %all-to-all-done = f32[16,128,4,8,9,2]{1,3,5,4,2,0:T(8,128)} async-done(((f32[16,128,4,8,9,2]{1,3,5,4,2,0:T(8,128)}), f32[16,128,4,8,9,2]{1,3,5,4,2,0:T(8,128)}, u32[]{:S(2)}, u32[]{:S(2)}) %all-to-all-start) | async-done | bytes 4718624 | tf_op jit(solution)/shard_map/all_to_all | solution.py:84
  137.1 6.3 %all-to-all-start.2 = ((f32[16,128,2,8,9,2]{1,3,5,4,2,0:T(8,128)}), f32[16,128,2,8,9,2]{1,3,5,4,2,0:T(8,128)S(1)}, u32[]{:S(2)}, u32[]{:S(2)}) async-start(f32[16,128,2,8,9,2]{1,3,5,4,2,0:T(8,128)} %copy.105), calls=%async_computation.2 | async-start | bytes 4718592 | tf_op jit(solution)/shard_map/all_to_all | solution.py:84
  144.7 5.2 %fusion.22 = f32[128,9,2,2,128]{4,0,1,3,2:T(8,128)S(1)} fusion(f32[16,128,2,8,9,2]{1,3,5,4,2,0:T(8,128)} %all-to-all-done.1, f32[16,8,1,128,1]{3,0,1,2,4:T(8,128)S(1)} %copy-done.6, f32[16,8,1,128,1]{3,0,1,2,4:T(8,128)S(1)} %get-tuple-element.46, f32[16,8,1,128,1]{3,0,1,2,4:T(8,128)S(1)} %get-tuple-element.45), kind=kOutput, calls=%fused_computation.41 | convolution fusion | flops 1812135936 | bytes 4915200 | tf_op jit(solution)/shard_map/spxyjt,syteu->ejuxp/dot_general | solution.py:87
  149.8 3.2 copy.102
  153.1 10.6 %gather_fusion.4 = f32[1024,2,2,128]{3,2,1,0:T(2,128)} fusion(f32[1152,2,2,128]{3,2,1,0:T(2,128)} %bitcast.196, s32[1024]{0:T(1024)S(1)} %broadcast_clamp_fusion), kind=kCustom, calls=%fused_computation.4 | custom fusion | bytes 4198400 | tf_op jit(solution)/shard_map/jit(_take)/gather | solution.py:89
  163.7 7.6 %add_reduce_fusion.2 = (f32[1024,128]{1,0:T(8,128)S(1)}, f32[1024,128]{1,0:T(8,128)S(1)}) fusion(f32[1024,2,2,128]{3,2,1,0:T(2,128)} %gather_fusion.4, f32[1024,2]{1,0:T(8,128)S(1)} %copy-done.4, f32[1024,2]{1,0:T(8,128)S(1)} %copy-done.5), kind=kLoop, calls=%fused_computation.59 | loop fusion | flops 1835008 | bytes 3162112 | tf_op jit(solution)/shard_map/reduce_sum | solution.py:94
  172.2 9.7 %fusion.11 = f32[128,9,2,4,128]{4,0,1,3,2:T(8,128)S(1)} fusion(f32[16,128,4,8,9,2]{1,3,5,4,2,0:T(8,128)} %all-to-all-done, f32[16,8,1,128,1]{3,0,1,2,4:T(8,128)S(1)} %copy-done.7, f32[16,8,1,128,1]{3,0,1,2,4:T(8,128)S(1)} %get-tuple-element.46, f32[16,8,1,128,1]{3,0,1,2,4:T(8,128)S(1)} %get-tuple-element.45), kind=kOutput, calls=%fused_computation.22 | convolution fusion | flops 3624075264 | bytes 9633792 | tf_op jit(solution)/shard_map/spxyjt,syteu->ejuxp/dot_general | solution.py:87
  181.9 5.2 %copy.107 = f32[128,9,2,4,128]{4,3,2,1,0:T(4,128)} copy(f32[128,9,2,4,128]{4,0,1,3,2:T(8,128)S(1)} %fusion.11) | data formatting | bytes 9437184 | tf_op jit(solution)/shard_map/spxyjt,syteu->ejuxp/transpose | solution.py:87
  187.1 11.8 %gather_fusion.7 = f32[1024,2,4,128]{3,2,1,0:T(4,128)} fusion(f32[1152,2,4,128]{3,2,1,0:T(4,128)} %bitcast.192, s32[1024]{0:T(1024)S(1)} %broadcast_clamp_fusion), kind=kCustom, calls=%fused_computation.7 | custom fusion | bytes 8392704 | tf_op jit(solution)/shard_map/jit(_take)/gather | solution.py:89
  198.9 8.1 %add_reduce_fusion = (f32[1024,128]{1,0:T(8,128)S(1)}, f32[1024,128]{1,0:T(8,128)S(1)}) fusion(f32[1024,2,4,128]{3,2,1,0:T(4,128)} %gather_fusion.7, f32[1024,4]{1,0:T(8,128)} %get-tuple-element.58, f32[1024,4]{1,0:T(8,128)} %get-tuple-element.59), kind=kLoop, calls=%fused_computation.38 | loop fusion | flops 3932160 | bytes 5275648 | tf_op jit(solution)/shard_map/reduce_sum | solution.py:94
  208.1 4.5 %fusion.25 = f32[128,9,2,2,128]{4,0,1,3,2:T(8,128)S(1)} fusion(f32[16,128,2,8,9,2]{1,3,5,4,2,0:T(8,128)S(1)} %all-to-all-done.2, f32[16,8,1,128,1]{3,0,1,2,4:T(8,128)} %get-tuple-element.47, f32[16,8,1,128,1]{3,0,1,2,4:T(8,128)S(1)} %get-tuple-element.46, f32[16,8,1,128,1]{3,0,1,2,4:T(8,128)S(1)} %get-tuple-element.45), kind=kOutput, calls=%fused_computation.42 | convolution fusion | flops 1812135936 | bytes 4915200 | tf_op jit(solution)/shard_map/spxyjt,syteu->ejuxp/dot_general | solution.py:87
  212.6 1.8 copy.110
  214.5 8.9 %gather_fusion.8 = f32[1024,2,2,128]{3,2,1,0:T(2,128)} fusion(f32[1152,2,2,128]{3,2,1,0:T(2,128)S(1)} %bitcast.195, s32[1024]{0:T(1024)S(1)} %broadcast_clamp_fusion), kind=kCustom, calls=%fused_computation.8 | custom fusion | bytes 4198400 | tf_op jit(solution)/shard_map/jit(_take)/gather | solution.py:89
  223.3 8.3 %add_reduce_fusion.1 = (f32[1024,128]{1,0:T(8,128)S(1)}, f32[1024,128]{1,0:T(8,128)S(1)}) fusion(f32[1024,2,2,128]{3,2,1,0:T(2,128)} %gather_fusion.8, f32[1024,2]{1,0:T(8,128)} %get-tuple-element.39, f32[1024,2]{1,0:T(8,128)} %get-tuple-element.57), kind=kLoop, calls=%fused_computation.57 | loop fusion | flops 1835008 | bytes 3162112 | tf_op jit(solution)/shard_map/reduce_sum | solution.py:94
  233.1 5.4 %all-to-all-start.3 = ((f32[8,128,2,128]{3,1,2,0:T(8,128)}), f32[8,128,2,128]{3,1,2,0:T(8,128)S(1)}, u32[]{:S(2)}, u32[]{:S(2)}) async-start(f32[8,128,2,128]{3,1,2,0:T(8,128)} %copy.112), calls=%async_computation.3 | async-start | bytes 2097152 | tf_op jit(solution)/shard_map/all_to_all | solution.py:103
  238.5 16.0 %all-to-all-done.3 = f32[8,128,2,128]{3,1,2,0:T(8,128)S(1)} async-done(((f32[8,128,2,128]{3,1,2,0:T(8,128)}), f32[8,128,2,128]{3,1,2,0:T(8,128)S(1)}, u32[]{:S(2)}, u32[]{:S(2)}) %all-to-all-start.3) | async-done | bytes 1048608 | tf_op jit(solution)/shard_map/all_to_all | solution.py:103
  254.5 2.7 collective-permute-start
  257.3 4.9 %collective-permute-done = f32[64,2,128]{2,0,1:T(8,128)S(1)} collective-permute-done((f32[64,2,128]{2,0,1:T(8,128)S(1)}, f32[64,2,128]{2,0,1:T(8,128)S(1)}, u32[]{:S(2)}, u32[]{:S(2)}) %collective-permute-start) | collective-permute-done | bytes 65568 | tf_op jit(solution)/shard_map/ppermute | solution.py:107
  263.7 6.6 %all-to-all-start.4 = ((f32[16,64,2,128]{3,2,1,0:T(2,128)}), f32[16,64,2,128]{3,2,1,0:T(2,128)S(1)}, u32[]{:S(2)}, u32[]{:S(2)}) async-start(f32[16,64,2,128]{3,2,1,0:T(2,128)} %broadcast_in_dim.77), calls=%async_computation.4 | async-start | bytes 2097152 | tf_op jit(solution)/shard_map/all_to_all | solution.py:110
  270.3 13.6 %all-to-all-done.4 = f32[16,64,2,128]{3,2,1,0:T(2,128)S(1)} async-done(((f32[16,64,2,128]{3,2,1,0:T(2,128)}), f32[16,64,2,128]{3,2,1,0:T(2,128)S(1)}, u32[]{:S(2)}, u32[]{:S(2)}) %all-to-all-start.4) | async-done | bytes 1048608 | tf_op jit(solution)/shard_map/all_to_all | solution.py:110
  283.9 4.7 %collective-permute-start.1 = (f32[512,2,128]{2,1,0:T(2,128)S(1)}, f32[512,2,128]{2,1,0:T(2,128)S(1)}, u32[]{:S(2)}, u32[]{:S(2)}) collective-permute-start(f32[512,2,128]{2,1,0:T(2,128)S(1)} %constant_dynamic-slice_fusion), channel_id=1, source_target_pairs={{0,0},{1,16},{2,32},{3,48},{4,64},{5,80},{6,96},{7,112},{8,1},{9,1... | collective-permute-start | bytes 1572872 | tf_op jit(solution)/shard_map/ppermute | solution.py:120
  289.6 45.2 %collective-permute-done.1 = f32[512,2,128]{2,1,0:T(2,128)S(1)} collective-permute-done((f32[512,2,128]{2,1,0:T(2,128)S(1)}, f32[512,2,128]{2,1,0:T(2,128)S(1)}, u32[]{:S(2)}, u32[]{:S(2)}) %collective-permute-start.1) | collective-permute-done | bytes 524320 | tf_op jit(solution)/shard_map/ppermute | solution.py:120
  335.1 1.8 fusion.84
  336.9 1.8 fusion.82
  338.7 1.8 fusion.83
  340.6 2.1 fusion.21
  342.7 2.0 copy-done.15
  (76 shorter events, 18.6 us)
Async XLA Ops:
  2.1 2.8 copy-start.2
  22.2 41.4 %all-to-all-start.1 = ((f32[16,128,2,8,9,2]{1,3,5,4,2,0:T(8,128)}), f32[16,128,2,8,9,2]{1,3,5,4,2,0:T(8,128)}, u32[]{:S(2)}, u32[]{:S(2)}) async-start(f32[16,128,2,8,9,2]{1,3,5,4,2,0:T(8,128)} %copy.100), calls=%async_computation.1 | async-start | bytes 4718592 | tf_op jit(solution)/shard_map/all_to_all | solution.py:84
  57.3 12.2 %copy-start.9 = (s32[8192]{0:T(1024)S(1)}, s32[8192]{0:T(1024)}, u32[]{:S(2)}) copy-start(s32[8192]{0:T(1024)} %param.14) | copy-start | bytes 98308
  63.6 73.5 %all-to-all-start = ((f32[16,128,4,8,9,2]{1,3,5,4,2,0:T(8,128)}), f32[16,128,4,8,9,2]{1,3,5,4,2,0:T(8,128)}, u32[]{:S(2)}, u32[]{:S(2)}) async-start(f32[16,128,4,8,9,2]{1,3,5,4,2,0:T(8,128)} %copy.98), calls=%async_computation | async-start | bytes 9437184 | tf_op jit(solution)/shard_map/all_to_all | solution.py:84
  69.7 2.0 copy-start
  71.7 2.0 copy-start.1
  137.1 71.0 %all-to-all-start.2 = ((f32[16,128,2,8,9,2]{1,3,5,4,2,0:T(8,128)}), f32[16,128,2,8,9,2]{1,3,5,4,2,0:T(8,128)S(1)}, u32[]{:S(2)}, u32[]{:S(2)}) async-start(f32[16,128,2,8,9,2]{1,3,5,4,2,0:T(8,128)} %copy.105), calls=%async_computation.2 | async-start | bytes 4718592 | tf_op jit(solution)/shard_map/all_to_all | solution.py:84
  143.4 1.3 copy-start.6
  153.1 10.6 %copy-start.4 = (f32[1024,2]{1,0:T(8,128)S(1)}, f32[1024,2]{1,0:T(8,128)}, u32[]{:S(2)}) copy-start(f32[1024,2]{1,0:T(8,128)} %get-tuple-element.40) | copy-start | bytes 24580
  153.1 10.6 %copy-start.5 = (f32[1024,2]{1,0:T(8,128)S(1)}, f32[1024,2]{1,0:T(8,128)}, u32[]{:S(2)}) copy-start(f32[1024,2]{1,0:T(8,128)} %get-tuple-element.56) | copy-start | bytes 24580
  171.3 0.8 copy-start.7
  223.3 8.3 %copy-start.3 = (f32[1024,2,128]{2,0,1:T(8,128)S(1)}, f32[1024,2,128]{2,0,1:T(8,128)}, u32[]{:S(2)}) copy-start(f32[1024,2,128]{2,0,1:T(8,128)} %pad_maximum_fusion.8) | copy-start | bytes 3145732
  233.1 21.3 %all-to-all-start.3 = ((f32[8,128,2,128]{3,1,2,0:T(8,128)}), f32[8,128,2,128]{3,1,2,0:T(8,128)S(1)}, u32[]{:S(2)}, u32[]{:S(2)}) async-start(f32[8,128,2,128]{3,1,2,0:T(8,128)} %copy.112), calls=%async_computation.3 | async-start | bytes 2097152 | tf_op jit(solution)/shard_map/all_to_all | solution.py:103
  254.5 7.7 %collective-permute-start = (f32[64,2,128]{2,0,1:T(8,128)S(1)}, f32[64,2,128]{2,0,1:T(8,128)S(1)}, u32[]{:S(2)}, u32[]{:S(2)}) collective-permute-start(f32[64,2,128]{2,0,1:T(8,128)S(1)} %dynamic-slice_bitcast_fusion), channel_id=1, source_target_pairs={{0,15},{1,14},{2,13},{3,12},{4,11},{5,10},{6,9},{7,8},{8,7},{9,6},... | collective-permute-start | bytes 196616 | tf_op jit(solution)/shard_map/ppermute | solution.py:107
  262.3 26.4 %copy-start.10 = (s32[128]{0:T(128)S(1)}, s32[128]{0:T(128)}, u32[]{:S(2)}) copy-start(s32[128]{0:T(128)} %param.12) | copy-start | bytes 1540
  262.3 26.4 %copy-start.11 = (s32[128]{0:T(128)S(1)}, s32[128]{0:T(128)}, u32[]{:S(2)}) copy-start(s32[128]{0:T(128)} %param.13) | copy-start | bytes 1540
  262.3 26.4 %copy-start.12 = (f32[64]{0:T(128)S(1)}, f32[64]{0:T(128)}, u32[]{:S(2)}) copy-start(f32[64]{0:T(128)} %param.10) | copy-start | bytes 772
  262.3 26.4 %copy-start.13 = (f32[64]{0:T(128)S(1)}, f32[64]{0:T(128)}, u32[]{:S(2)}) copy-start(f32[64]{0:T(128)} %param.11) | copy-start | bytes 772
  263.7 20.2 %all-to-all-start.4 = ((f32[16,64,2,128]{3,2,1,0:T(2,128)}), f32[16,64,2,128]{3,2,1,0:T(2,128)S(1)}, u32[]{:S(2)}, u32[]{:S(2)}) async-start(f32[16,64,2,128]{3,2,1,0:T(2,128)} %broadcast_in_dim.77), calls=%async_computation.4 | async-start | bytes 2097152 | tf_op jit(solution)/shard_map/all_to_all | solution.py:110
  283.9 50.8 %collective-permute-start.1 = (f32[512,2,128]{2,1,0:T(2,128)S(1)}, f32[512,2,128]{2,1,0:T(2,128)S(1)}, u32[]{:S(2)}, u32[]{:S(2)}) collective-permute-start(f32[512,2,128]{2,1,0:T(2,128)S(1)} %constant_dynamic-slice_fusion), channel_id=1, source_target_pairs={{0,0},{1,16},{2,32},{3,48},{4,64},{5,80},{6,96},{7,112},{8,1},{9,1... | collective-permute-start | bytes 1572872 | tf_op jit(solution)/shard_map/ppermute | solution.py:120
  335.1 5.4 %copy-start.14 = (f32[2,1024,512]{2,1,0:T(8,128)S(1)}, f32[2,1024,512]{2,1,0:T(8,128)}, u32[]{:S(2)}) copy-start(f32[2,1024,512]{2,1,0:T(8,128)} %custom-call.18) | copy-start | bytes 12582916
  336.9 3.6 %copy-start.8 = (f32[2,1024,512]{2,1,0:T(8,128)S(1)}, f32[2,1024,512]{2,1,0:T(8,128)}, u32[]{:S(2)}) copy-start(f32[2,1024,512]{2,1,0:T(8,128)} %param.15) | copy-start | bytes 12582916
  342.7 2.0 copy-start.15
